TPU v7x, 32 devices: a whole 2x2x4 slice. The times are simulated.
32 devices in a mesh: ctx: 4 (over y, x), tp: 8 (over z, core).
Axes of the slice: x: 2, y: 2, z: 4, core: 2. Of those that a mesh axis runs over, the one named last changes fastest.
Arguments:
- resid: bfloat16 [1024, 4096], P('ctx', 'tp'), may hold values from -6 to 6
- attn_gain: bfloat16 [4096], replicated, may hold values from 0.5 to 1.5
- mlp_gain: bfloat16 [4096], replicated, may hold values from 0.5 to 1.5
- w_query: bfloat16 [4096, 4096], P(None, 'tp'), may hold values from -0.09375 to 0.09375
- w_kv: bfloat16 [4096, 1024], P(None, 'tp'), may hold values from -0.09375 to 0.09375
- w_out: bfloat16 [4096, 4096], P('tp'), may hold values from -0.09375 to 0.09375
- w_gate: bfloat16 [4096, 11008], P(None, 'tp'), may hold values from -0.09375 to 0.09375
- w_up: bfloat16 [4096, 11008], P(None, 'tp'), may hold values from -0.09375 to 0.09375
- w_down: bfloat16 [11008, 4096], P('tp'), may hold values from -0.0546875 to 0.0546875
- kv_cache: bfloat16 [32, 128, 1024], P('ctx'), may hold values from -70 to 70
- cache_len: int32 [4], replicated, may hold values from 1 to 2048
- span_len: int32 [4], replicated, may hold values from 1 to 256
- slot_req: int32 [32], P('ctx'), may hold values from 0 to 4, as said below
- slot_blk: int32 [32], P('ctx'), may hold values from 0 to 15, as said below
Outputs:
- layer_out: bfloat16 [1024, 4096], P('ctx', 'tp')
- new_kv: bfloat16 [1024, 1024], P('ctx', 'tp')
Inputs may be any that keep to these rules, and one draw needn't show every extreme that they name: `slot_req`: each request r holds ceil(cache_len[r] / 128) blocks, and each of its blocks stands in exactly one slot; every other slot is empty. `slot_blk`: block numbers of live slots are below their request's block count; empty slots carry 0.
All inputs are finite; a program needn't handle non-finite values.
Results may differ from a plain program's by a relative error of at most 0.035.
Values may be sent and summed in bfloat16 or wider, within the bound.
No kernel may reach another device: no remote copies, remote signals or barrier semaphores. Data moves between devices by JAX's collectives and lax.ppermute only.
A program may use at most 128 MiB of HBM per device.

v0:
```python
import jax
import jax.numpy as jnp
from jax import lax
from jax.sharding import PartitionSpec as P

HQ = 32
KVH = 4
HD = 128
BLK = 128
THETA = 5000000.0
EPS = 1e-05
NEG = -1e30


def rms_norm(values, gain):
    wide = values.astype(jnp.float32)
    factor = lax.rsqrt(jnp.mean(wide * wide, axis=-1, keepdims=True) + EPS)
    return (wide * factor * gain.astype(jnp.float32)).astype(jnp.bfloat16)


def rotate(vectors, positions):
    width = vectors.shape[-1]
    half = width // 2
    freqs = THETA ** (-(jnp.arange(half, dtype=jnp.float32) * 2.0 / width))
    angles = positions.astype(jnp.float32)[:, None] * freqs[None, :]
    cosine = jnp.cos(angles)[:, None, :]
    sine = jnp.sin(angles)[:, None, :]
    first = vectors[..., :half]
    second = vectors[..., half:]
    return jnp.concatenate(
        [first * cosine - second * sine, second * cosine + first * sine], axis=-1
    )


def column_term(rows, weight):
    return lax.dot_general(
        weight, rows, (((0,), (1,)), ((), ())), preferred_element_type=jnp.float32
    )


def gather_ctx(value, count):
    parts = [value]
    for shift in range(1, count):
        pairs = [(i, (i + shift) % count) for i in range(count)]
        parts.append(lax.ppermute(value, "ctx", pairs))
    return parts


def per_device(
    resid,
    attn_gain,
    mlp_gain,
    w_query,
    w_kv,
    w_out,
    w_gate,
    w_up,
    w_down,
    kv_cache,
    cache_len,
    span_len,
    slot_req,
    slot_blk,
):
    span_size = resid.shape[0]
    ctx_count = lax.axis_size("ctx")
    q_cols = w_query.shape[1]
    heads_dev = q_cols // HD
    ctx_rank = lax.axis_index("ctx")
    tp_rank = lax.axis_index("tp")
    group = tp_rank * heads_dev // (HQ // KVH)
    my_len = cache_len[ctx_rank]
    my_span = span_len[ctx_rank]
    offsets = jnp.arange(span_size, dtype=jnp.int32)
    positions = my_len + offsets
    live_rows = offsets < my_span
    own_cache = jnp.concatenate(
        [
            lax.dynamic_slice_in_dim(kv_cache, group * HD, HD, 2),
            lax.dynamic_slice_in_dim(kv_cache, KVH * HD + group * HD, HD, 2),
        ],
        axis=2,
    )
    own_meta = jnp.stack([slot_req, slot_blk])
    cache_all = jnp.concatenate(gather_ctx(own_cache, ctx_count), axis=0)
    meta_all = jnp.concatenate(gather_ctx(own_meta, ctx_count), axis=1)
    full_resid = lax.all_gather(resid, "tp", axis=1, tiled=True)
    x_norm = rms_norm(full_resid, attn_gain)
    query = rotate(
        jnp.dot(x_norm, w_query, preferred_element_type=jnp.float32).reshape(
            span_size, heads_dev, HD
        ),
        positions,
    ).astype(jnp.bfloat16)
    kv_piece = jnp.dot(x_norm, w_kv, preferred_element_type=jnp.float32).astype(jnp.bfloat16)
    kv_width = kv_piece.shape[1]
    kv_all = lax.all_gather(kv_piece, "tp", axis=1, tiled=True)
    all_keys = rotate(
        kv_all[:, : KVH * HD].astype(jnp.float32).reshape(span_size, KVH, HD), positions
    ).astype(jnp.bfloat16)
    joined = jnp.concatenate([all_keys.reshape(span_size, KVH * HD), kv_all[:, KVH * HD :]], axis=1)
    mine = lax.dynamic_slice_in_dim(joined, tp_rank * kv_width, kv_width, 1)
    new_kv = jnp.where(live_rows[:, None], mine, jnp.zeros_like(mine))
    new_keys = lax.dynamic_index_in_dim(all_keys, group, 1, keepdims=False)
    new_vals = lax.dynamic_slice_in_dim(kv_all, KVH * HD + group * HD, HD, 1)
    cache_rows = cache_all.shape[0] * BLK
    keys = jnp.concatenate([cache_all[..., :HD].reshape(cache_rows, HD), new_keys], axis=0)
    vals = jnp.concatenate([cache_all[..., HD:].reshape(cache_rows, HD), new_vals], axis=0)
    key_pos = meta_all[1][:, None] * BLK + jnp.arange(BLK, dtype=jnp.int32)[None, :]
    cache_ok = ((meta_all[0][:, None] == ctx_rank) & (key_pos < my_len)).reshape(cache_rows)
    new_ok = (offsets[None, :] <= offsets[:, None]) & (offsets[None, :] < my_span)
    valid = jnp.concatenate(
        [jnp.broadcast_to(cache_ok[None, :], (span_size, cache_rows)), new_ok], axis=1
    )
    scores = jnp.einsum("chd,kd->hck", query, keys, preferred_element_type=jnp.float32) * HD ** (
        -0.5
    )
    peak = jnp.max(jnp.where(valid[None], scores, NEG), axis=2)
    weights = jnp.where(valid[None], jnp.exp(scores - peak[..., None]), 0.0)
    total = jnp.sum(weights, axis=2)
    summed = jnp.einsum(
        "hck,kd->hcd", weights.astype(jnp.bfloat16), vals, preferred_element_type=jnp.float32
    )
    attn_rows = (
        (summed / total[..., None])
        .transpose(1, 0, 2)
        .reshape(span_size, q_cols)
        .astype(jnp.bfloat16)
    )
    head_sum = lax.psum(
        jnp.dot(attn_rows, w_out, preferred_element_type=jnp.float32).astype(jnp.bfloat16), "tp"
    )
    full_mid = (full_resid.astype(jnp.float32) + head_sum.astype(jnp.float32)).astype(jnp.bfloat16)
    mid = lax.dynamic_slice_in_dim(full_mid, tp_rank * resid.shape[1], resid.shape[1], 1)
    x_two = rms_norm(full_mid, mlp_gain)
    gate = jnp.dot(x_two, w_gate, preferred_element_type=jnp.float32)
    up_part = jnp.dot(x_two, w_up, preferred_element_type=jnp.float32)
    hidden = (jax.nn.silu(gate) * up_part).astype(jnp.bfloat16)
    down_sum = lax.psum_scatter(
        column_term(hidden, w_down).astype(jnp.bfloat16), "tp", scatter_dimension=0, tiled=True
    ).astype(jnp.float32)
    layer_out = (mid.astype(jnp.float32) + down_sum.T).astype(jnp.bfloat16)
    layer_out = jnp.where(live_rows[:, None], layer_out, jnp.zeros_like(layer_out))
    return (layer_out, new_kv)


def solution(mesh):
    return jax.shard_map(
        per_device,
        mesh=mesh,
        in_specs=(
            P("ctx", "tp"),
            P(),
            P(),
            P(None, "tp"),
            P(None, "tp"),
            P("tp", None),
            P(None, "tp"),
            P(None, "tp"),
            P("tp", None),
            P("ctx", None, None),
            P(),
            P(),
            P("ctx"),
            P("ctx"),
        ),
        out_specs=(P("ctx", "tp"), P("ctx", "tp")),
        check_vma=False,
    )
```

profile of v0, /device:TPU:0, one launch (start us, length us, event | category | flops | bytes accessed | tf_op | source)
XLA Modules:
  0.0 248.4 jit_solution(2127436485068741131)
XLA Ops:
  8.6 3.9 %collective-permute-start.2 = (s32[2,8]{1,0:T(2,128)S(1)}, s32[2,8]{1,0:T(2,128)S(1)}, u32[]{:S(2)}, u32[]{:S(2)}) collective-permute-start(s32[2,8]{1,0:T(2,128)S(1)} %pad_add_fusion.1), channel_id=1, source_target_pairs={{0,24},{8,0},{16,8},{24,16},{1,25},{9,1},{17,9},{25,17},{2,26},{10... | collective-permute-start | bytes 200 | tf_op jit(solution)/shard_map/ppermute | solution.py:45
  13.6 1.1 constant_dynamic-slice_fusion.2
  14.8 2.4 collective-permute-start.5
  17.2 1.5 collective-permute-start.4
  18.7 1.2 dynamic_slice.25
  19.9 1.3 dynamic_slice.26
  23.3 1.2 multiply_cosine_fusion
  24.5 0.8 pad_add_fusion.2
  26.0 5.1 %pad_add_fusion = pred[256,4352]{0,1:T(8,128)(4,1)} fusion(pred[256,256]{0,1:T(8,128)(4,1)S(1)} %fusion.45, pred[4352]{0:T(1024)(128)(4,1)S(1)} %pad.8.clone), kind=kLoop, calls=%fused_computation.20 | loop fusion | flops 1114112 | bytes 1184000 | tf_op jit(solution)/shard_map/concatenate | solution.py:112
  31.1 9.8 %collective-permute-done.4 = bf16[8,128,256]{2,1,0:T(8,128)(2,1)S(1)} collective-permute-done((bf16[8,128,256]{2,1,0:T(8,128)(2,1)S(1)}, bf16[8,128,256]{2,1,0:T(8,128)(2,1)S(1)}, u32[]{:S(2)}, u32[]{:S(2)}) %collective-permute-start.4) | collective-permute-done | bytes 524320 | tf_op jit(solution)/shard_map/ppermute | solution.py:45
  41.2 1.6 fusion.56
  42.8 1.3 copy.25
  44.1 2.2 fusion.14
  46.3 2.4 convolution_convert_fusion.2
  48.7 14.3 %all_gather.7 = bf16[256,1024]{1,0:T(8,128)(2,1)S(1)} all-gather(bf16[256,128]{1,0:T(8,128)(2,1)S(1)} %convolution_convert_fusion.2), channel_id=1, replica_groups=mesh['ctx'=4,'tp'=8] {'tp'}, dimensions={1}, use_global_device_ids=true | all-gather | bytes 589824 | tf_op jit(solution)/shard_map/all_gather | solution.py:97
  63.0 0.9 fusion.57
  63.9 0.7 copy.21
  64.7 3.5 %fusion.37 = f32[256,512]{1,0:T(8,128)S(1)} fusion(bf16[4096,512]{1,0:T(8,128)(2,1)} %param.17, bf16[256,4096]{1,0:T(8,128)(2,1)S(1)} %copy-done.2, f32[4096]{0:T(1024)S(1)} %convert_element_type.74, f32[256]{0:T(256)S(1)} %add_rsqrt_fusion.1), kind=kOutput, calls=%fused_computation.43 | convolution fusion | flops 1077936128 | bytes 6833152 | tf_op jit(solution)/shard_map/dot_general | solution.py:90
  68.4 1.2 reshape.161
  70.3 1.0 multiply_subtract_fusion
  71.5 1.0 subtract_convert_fusion
  72.6 8.7 %fusion.30 = f32[4352,256,4]{1,0,2:T(8,128)} fusion(bf16[256,128]{1,0:T(8,128)(2,1)S(1)} %dynamic-slice_bitcast_fusion, bf16[4096,128]{1,0:T(8,128)(2,1)S(1)} %bitcast.63, bf16[256,4,64]{2,0,1:T(8,128)(2,1)S(1)} %get-tuple-element.9, bf16[256,4,64]{2,0,1:T(8,128)(2,1)S(1)} %get-tuple-element.8), kind=kOutput, calls=%fused_computation.39 | convolution fusion | flops 1143603200 | bytes 19202048 | tf_op jit(solution)/shard_map/chd,kd->hck/dot_general | solution.py:115
  81.2 18.7 %fusion.60 = (f32[4,256]{1,0:T(4,128)S(1)}, bf16[4,256,4352]{1,2,0:T(8,128)(2,1)}) fusion(f32[4352,256,4]{1,0,2:T(8,128)} %fusion.30, pred[256,4352]{0,1:T(8,128)(4,1)} %pad_add_fusion), kind=kOutput, calls=%fused_computation.91 | output fusion | flops 31199488 | bytes 27856896 | tf_op jit(solution)/shard_map/sub | solution.py:119
  100.0 5.3 %fusion.25 = bf16[256,4,128]{0,2,1:T(8,128)(2,1)S(1)} fusion(bf16[4,256,4352]{1,2,0:T(8,128)(2,1)} %get-tuple-element.21, bf16[256,128]{0,1:T(8,128)(2,1)S(1)} %copy-done.8, bf16[4096,128]{0,1:T(8,128)(2,1)} %copy.25, f32[256,4]{0,1:T(4,128)S(1)} %bitcast.70), kind=kOutput, calls=%fused_computation.33 | convolution fusion | flops 1143341056 | bytes 10293248 | tf_op jit(solution)/shard_map/hck,kd->hcd/dot_general | solution.py:121
  105.3 2.7 %convolution_convert_fusion = bf16[256,4096]{1,0:T(8,128)(2,1)} fusion(bf16[256,512]{0,1:T(8,128)(2,1)S(1)} %bitcast.65, bf16[512,4096]{1,0:T(8,128)(2,1)S(1)} %copy-done.3), kind=kOutput, calls=%fused_computation.17 | convolution fusion | flops 1074790400 | bytes 6553600 | tf_op jit(solution)/shard_map/dot_general | solution.py:131
  108.1 63.7 %all-reduce.2.cloned.1.call-done = bf16[256,4096]{1,0:T(8,128)(2,1)} async-done(((bf16[256,4096]{1,0:T(8,128)(2,1)}), bf16[256,4096]{1,0:T(8,128)(2,1)}) %all-reduce.2.cloned.1.call-update) | async-done | bytes 2097168 | tf_op jit(solution)/shard_map/psum | solution.py:130
  171.8 3.9 %fusion.11 = (f32[256]{0:T(256)S(1)}, bf16[256,4096]{1,0:T(8,128)(2,1)}) fusion(bf16[256,4096]{1,0:T(8,128)(2,1)} %all-reduce.2.cloned.1.call-done, bf16[256,4096]{1,0:T(8,128)(2,1)S(1)} %copy-done.2), kind=kLoop, calls=%fused_computation.21 | loop fusion | flops 7339776 | bytes 6292480 | tf_op jit(solution)/shard_map/reduce_sum | solution.py:17
  175.7 7.0 %fusion.35 = f32[256,1376]{0,1:T(8,128)S(1)} fusion(bf16[4096,1376]{0,1:T(8,128)(2,1)} %param.20, bf16[256,4096]{1,0:T(8,128)(2,1)} %get-tuple-element.3, f32[4096]{0:T(1024)S(1)} %convert_element_type.87, f32[256]{0:T(256)S(1)} %add_rsqrt_fusion), kind=kOutput, calls=%fused_computation.42 | convolution fusion | flops 2889875456 | bytes 14795776 | tf_op jit(solution)/shard_map/dot_general | solution.py:136
  182.7 21.7 %fusion.10 = bf16[4096,256]{0,1:T(8,128)(2,1)} fusion(bf16[1376,4096]{1,0:T(8,128)(2,1)} %param.22, bf16[4096,1376]{0,1:T(8,128)(2,1)} %param.21, f32[256,1376]{0,1:T(8,128)S(1)} %fusion.35, bf16[256,4096]{1,0:T(8,128)(2,1)} %get-tuple-element.3, f32[4096]{0:T(1024)S(1)} %convert_element_type.87, f32[256]{0:T(256)S(1)} %add_rsqrt_fusion), kind=kOutput, calls=%fused_computation.19 | convolution fusion | flops 5778718720 | bytes 28165120 | tf_op jit(solution)/shard_map/dot_general | solution.py:36
  204.6 0.7 fusion.47
  205.4 34.7 %reduce-scatter.2.cloned.1.call-done = bf16[512,256]{0,1:T(8,128)(2,1)} async-done(((bf16[4096,256]{0,1:T(8,128)(2,1)}), bf16[512,256]{0,1:T(8,128)(2,1)}) %reduce-scatter.2.cloned.1.call-update) | async-done | bytes 262160 | tf_op jit(solution)/shard_map/reduce_scatter | solution.py:139
  240.1 1.8 fusion.41
  (57 shorter events, 7.1 us)
Async XLA Ops:
  7.2 39.1 %copy-start = (bf16[4096,128]{1,0:T(8,128)(2,1)S(1)}, bf16[4096,128]{1,0:T(8,128)(2,1)}, u32[]{:S(2)}) copy-start(bf16[4096,128]{1,0:T(8,128)(2,1)} %param.18) | copy-start | bytes 3145732
  7.2 36.9 %all-gather.2.cloned.1.call-start = ((), (), s32[]{:S(2)}) async-start(), calls=%async_computation.1 | async-start | bytes 2359296 | tf_op jit(solution)/shard_map/all_gather | solution.py:87
  7.9 163.9 %all-reduce.2.cloned.1.call-start = ((), (), s32[]{:S(2)}) async-start(), calls=%async_computation.2 | async-start | bytes 4194304 | tf_op jit(solution)/shard_map/psum | solution.py:130
  8.6 15.9 %collective-permute-start.2 = (s32[2,8]{1,0:T(2,128)S(1)}, s32[2,8]{1,0:T(2,128)S(1)}, u32[]{:S(2)}, u32[]{:S(2)}) collective-permute-start(s32[2,8]{1,0:T(2,128)S(1)} %pad_add_fusion.1), channel_id=1, source_target_pairs={{0,24},{8,0},{16,8},{24,16},{1,25},{9,1},{17,9},{25,17},{2,26},{10... | collective-permute-start | bytes 200 | tf_op jit(solution)/shard_map/ppermute | solution.py:45
  12.5 12.0 %collective-permute-start.1 = (s32[2,8]{1,0:T(2,128)S(1)}, s32[2,8]{1,0:T(2,128)S(1)}, u32[]{:S(2)}, u32[]{:S(2)}) collective-permute-start(s32[2,8]{1,0:T(2,128)S(1)} %pad_add_fusion.1), channel_id=1, source_target_pairs={{0,16},{8,24},{16,0},{24,8},{1,17},{9,25},{17,1},{25,9},{2,18},{10... | collective-permute-start | bytes 200 | tf_op jit(solution)/shard_map/ppermute | solution.py:45
  13.0 11.5 %collective-permute-start = (s32[2,8]{1,0:T(2,128)S(1)}, s32[2,8]{1,0:T(2,128)S(1)}, u32[]{:S(2)}, u32[]{:S(2)}) collective-permute-start(s32[2,8]{1,0:T(2,128)S(1)} %pad_add_fusion.1), channel_id=1, source_target_pairs={{0,8},{8,16},{16,24},{24,0},{1,9},{9,17},{17,25},{25,1},{2,10},{10... | collective-permute-start | bytes 200 | tf_op jit(solution)/shard_map/ppermute | solution.py:45
  14.8 16.4 %collective-permute-start.5 = (bf16[8,128,256]{2,1,0:T(8,128)(2,1)S(1)}, bf16[8,128,256]{2,1,0:T(8,128)(2,1)S(1)}, u32[]{:S(2)}, u32[]{:S(2)}) collective-permute-start(bf16[8,128,256]{2,1,0:T(8,128)(2,1)S(1)} %pad_maximum_fusion.1), channel_id=1, source_target_pairs={{0,24},{8,0},{16,8},{24,16},{1,25},{9,1},{17,9},{25,17},{2,26},{10... | collective-permute-start | bytes 1572872 | tf_op jit(solution)/shard_map/ppermute | solution.py:45
  17.2 23.8 %collective-permute-start.4 = (bf16[8,128,256]{2,1,0:T(8,128)(2,1)S(1)}, bf16[8,128,256]{2,1,0:T(8,128)(2,1)S(1)}, u32[]{:S(2)}, u32[]{:S(2)}) collective-permute-start(bf16[8,128,256]{2,1,0:T(8,128)(2,1)S(1)} %pad_maximum_fusion.1), channel_id=1, source_target_pairs={{0,16},{8,24},{16,0},{24,8},{1,17},{9,25},{17,1},{25,9},{2,18},{10... | collective-permute-start | bytes 1572872 | tf_op jit(solution)/shard_map/ppermute | solution.py:45
  24.5 16.4 %collective-permute-start.3 = (bf16[8,128,256]{2,1,0:T(8,128)(2,1)S(1)}, bf16[8,128,256]{2,1,0:T(8,128)(2,1)S(1)}, u32[]{:S(2)}, u32[]{:S(2)}) collective-permute-start(bf16[8,128,256]{2,1,0:T(8,128)(2,1)S(1)} %pad_maximum_fusion.1), channel_id=1, source_target_pairs={{0,8},{8,16},{16,24},{24,0},{1,9},{9,17},{17,25},{25,1},{2,10},{10... | collective-permute-start | bytes 1572872 | tf_op jit(solution)/shard_map/ppermute | solution.py:45
  44.1 20.6 %copy-start.2 = (bf16[256,4096]{1,0:T(8,128)(2,1)S(1)}, bf16[256,4096]{1,0:T(8,128)(2,1)}, u32[]{:S(2)}) copy-start(bf16[256,4096]{1,0:T(8,128)(2,1)} %all-gather.2.cloned.1.call-done) | copy-start | bytes 6291460
  69.6 3.0 %copy-start.4 = (bf16[32,128,128]{2,1,0:T(8,128)(2,1)S(1)}, bf16[32,128,128]{2,1,0:T(8,128)(2,1)}, u32[]{:S(2)}) copy-start(bf16[32,128,128]{2,1,0:T(8,128)(2,1)} %get-tuple-element.5) | copy-start | bytes 3145732
  71.3 9.9 %copy-start.5 = (bf16[256,4,64]{2,0,1:T(8,128)(2,1)}, bf16[256,4,64]{2,0,1:T(8,128)(2,1)S(1)}, u32[]{:S(2)}) copy-start(bf16[256,4,64]{2,0,1:T(8,128)(2,1)S(1)} %get-tuple-element.11) | copy-start | bytes 393220
  81.2 18.7 %copy-start.8 = (bf16[256,128]{0,1:T(8,128)(2,1)S(1)}, bf16[256,128]{0,1:T(8,128)(2,1)}, u32[]{:S(2)}) copy-start(bf16[256,128]{0,1:T(8,128)(2,1)} %copy.21) | copy-start | bytes 196612
  100.0 5.3 %copy-start.3 = (bf16[512,4096]{1,0:T(8,128)(2,1)S(1)}, bf16[512,4096]{1,0:T(8,128)(2,1)}, u32[]{:S(2)}) copy-start(bf16[512,4096]{1,0:T(8,128)(2,1)} %param.19) | copy-start | bytes 12582916
  105.3 2.7 %copy-start.9 = (bf16[4096]{0:T(1024)(128)(2,1)S(1)}, bf16[4096]{0:T(1024)(128)(2,1)}, u32[]{:S(2)}) copy-start(bf16[4096]{0:T(1024)(128)(2,1)} %param.16) | copy-start | bytes 24580
  108.0 132.1 %reduce-scatter.2.cloned.1.call-start = ((), (), s32[]{:S(2)}) async-start(), calls=%async_computation.3 | async-start | bytes 2359296 | tf_op jit(solution)/shard_map/reduce_scatter | solution.py:139
  182.7 21.8 %copy-start.6 = (bf16[256,4,64]{2,0,1:T(8,128)(2,1)S(1)}, bf16[256,4,64]{2,0,1:T(8,128)(2,1)}, u32[]{:S(2)}) copy-start(bf16[256,4,64]{2,0,1:T(8,128)(2,1)} %copy-done.5) | copy-start | bytes 393220
  182.7 21.9 %copy-start.7 = (bf16[256,512]{1,0:T(8,128)(2,1)S(1)}, bf16[256,512]{1,0:T(8,128)(2,1)}, u32[]{:S(2)}) copy-start(bf16[256,512]{1,0:T(8,128)(2,1)} %get-tuple-element.12) | copy-start | bytes 786436
  182.7 59.2 %copy-start.1 = (bf16[4096,128]{1,0:T(8,128)(2,1)S(1)}, bf16[4096,128]{1,0:T(8,128)(2,1)}, u32[]{:S(2)}) copy-start(bf16[4096,128]{1,0:T(8,128)(2,1)} %param.18) | copy-start | bytes 3145732
Sparse Core Ops, SparseCore 0:
  9.6 31.7 all-gather.1
  108.1 63.6 all-reduce.1
  204.6 35.4 reduce-scatter.1
where the time goes:
time: 249 us; the launch traced here: 248 us
  waiting for transfers between devices  109 us (44%)
  matrix products  51.2 us (21%)
  other arithmetic  41.7 us (17%)
  blocking collectives  14.3 us (6%)
  between operations  14 us (6%)
  local copies, waits for them, and re-layouts  9.32 us (4%)
  starting transfers between devices  9.02 us (4%)
    psum x1, waiting for transfers between devices, per_device(): lax.psum(jnp.dot(attn_rows, w_out, preferred_element_type=jnp.float32).as...  63.7 us
    reduce_scatter x1, waiting for transfers between devices, per_device(): lax.psum_scatter(column_term(hidden, w_down).astype(jnp.bfloat16), 'tp',...  34.7 us
    dot_general x1, matrix products, column_term(): lax.dot_general(weight, rows, (((0,), (1,)), ((), ())), preferred_element...  21.7 us
    sub x1, other arithmetic, per_device(): weights = jnp.where(valid[None], jnp.exp(scores - peak[..., None]), 0.0)  18.7 us
    all_gather x1, blocking collectives, per_device(): kv_all = lax.all_gather(kv_piece, 'tp', axis=1, tiled=True)  14.3 us
    ppermute x6, waiting for transfers between devices, gather_ctx(): parts.append(lax.ppermute(value, 'ctx', pairs))  9.82 us
    ppermute x6, starting transfers between devices, gather_ctx(): parts.append(lax.ppermute(value, 'ctx', pairs))  8.9 us
    dot_general x1, matrix products, per_device(): jnp.einsum('chd,kd->hck', query, keys, preferred_element_type=jnp.float32)  8.67 us
  transfers between devices with their start and end apart: 9, of which 3 were waited for; matrix products, arithmetic and copies ran while one was open for 7% of the time, Pallas kernels for 0%

commit v1 on v0

--- a/solution.py
+++ b/solution.py
@@ -127,8 +127,12 @@
         .reshape(span_size, q_cols)
         .astype(jnp.bfloat16)
     )
-    head_sum = lax.psum(
-        jnp.dot(attn_rows, w_out, preferred_element_type=jnp.float32).astype(jnp.bfloat16), "tp"
+
+    def _perform_fields(state):
+        return lax.all_gather(state, "tp").sum(axis=0)
+
+    head_sum = _perform_fields(
+        jnp.dot(attn_rows, w_out, preferred_element_type=jnp.float32).astype(jnp.bfloat16)
     )
     full_mid = (full_resid.astype(jnp.float32) + head_sum.astype(jnp.float32)).astype(jnp.bfloat16)
     mid = lax.dynamic_slice_in_dim(full_mid, tp_rank * resid.shape[1], resid.shape[1], 1)

time: 249 us -> 344 us (1.38)
  waiting for transfers between devices: 109 us -> 194 us
  other arithmetic: 41.7 us -> 50.9 us
    all_gather x0 -> x1, waiting for transfers between devices: none -> 150 us  [_perform_fields(): return lax.all_gather(state, 'tp').sum(axis=0)]
    psum x1 -> x0, waiting for transfers between devices: 63.7 us -> none  [per_device(): lax.psum(jnp.dot(attn_rows, w_out, preferred_element_type=jnp.float32).as...]
    reduce_sum x0 -> x1, other arithmetic: none -> 10.5 us  [_perform_fields(): return lax.all_gather(state, 'tp').sum(axis=0)]
  transfers between devices with their start and end apart: 9 -> 9, of which waited for: 3 -> 3; matrix products, arithmetic and copies ran while one was open for 7% -> 5% of each run, Pallas kernels for 0% -> 0%
where the time goes in v1:
time: 344 us; the launch traced here: 343 us
  waiting for transfers between devices  194 us (56%)
  other arithmetic  50.9 us (15%)
  matrix products  50.6 us (15%)
  blocking collectives  14.3 us (4%)
  between operations  14 us (4%)
  local copies, waits for them, and re-layouts  10.7 us (3%)
  starting transfers between devices  9.02 us (3%)
    all_gather x1, waiting for transfers between devices, _perform_fields(): return lax.all_gather(state, 'tp').sum(axis=0)  150 us
    reduce_scatter x1, waiting for transfers between devices, per_device(): lax.psum_scatter(column_term(hidden, w_down).astype(jnp.bfloat16), 'tp',...  33.3 us
    dot_general x1, matrix products, column_term(): lax.dot_general(weight, rows, (((0,), (1,)), ((), ())), preferred_element...  21.7 us
    sub x1, other arithmetic, per_device(): weights = jnp.where(valid[None], jnp.exp(scores - peak[..., None]), 0.0)  18.8 us
    all_gather x1, blocking collectives, per_device(): kv_all = lax.all_gather(kv_piece, 'tp', axis=1, tiled=True)  14.3 us
    reduce_sum x1, other arithmetic, _perform_fields(): return lax.all_gather(state, 'tp').sum(axis=0)  10.5 us
    ppermute x6, waiting for transfers between devices, gather_ctx(): parts.append(lax.ppermute(value, 'ctx', pairs))  9.8 us
    ppermute x6, starting transfers between devices, gather_ctx(): parts.append(lax.ppermute(value, 'ctx', pairs))  8.9 us
  transfers between devices with their start and end apart: 9, of which 3 were waited for; matrix products, arithmetic and copies ran while one was open for 5% of the time, Pallas kernels for 0%

profile of v1, /device:TPU:0, one launch (start us, length us, event | category | flops | bytes accessed | tf_op | source)
XLA Modules:
  0.0 343.1 jit_solution(17031306400249498253)
XLA Ops:
  8.6 3.9 %collective-permute-start.2 = (s32[2,8]{1,0:T(2,128)S(1)}, s32[2,8]{1,0:T(2,128)S(1)}, u32[]{:S(2)}, u32[]{:S(2)}) collective-permute-start(s32[2,8]{1,0:T(2,128)S(1)} %pad_add_fusion.1), channel_id=1, source_target_pairs={{0,24},{8,0},{16,8},{24,16},{1,25},{9,1},{17,9},{25,17},{2,26},{10... | collective-permute-start | bytes 200 | tf_op jit(solution)/shard_map/ppermute | solution.py:45
  13.6 1.1 constant_dynamic-slice_fusion.2
  14.8 2.4 collective-permute-start.5
  17.2 1.5 collective-permute-start.4
  18.7 1.2 dynamic_slice.25
  19.9 1.3 dynamic_slice.26
  23.3 1.2 multiply_cosine_fusion
  24.5 0.8 pad_add_fusion.2
  26.0 5.1 %pad_add_fusion = pred[256,4352]{0,1:T(8,128)(4,1)} fusion(pred[256,256]{0,1:T(8,128)(4,1)S(1)} %fusion.45, pred[4352]{0:T(1024)(128)(4,1)S(1)} %pad.8.clone), kind=kLoop, calls=%fused_computation.20 | loop fusion | flops 1114112 | bytes 1184000 | tf_op jit(solution)/shard_map/concatenate | solution.py:112
  31.2 9.8 %collective-permute-done.4 = bf16[8,128,256]{2,1,0:T(8,128)(2,1)S(1)} collective-permute-done((bf16[8,128,256]{2,1,0:T(8,128)(2,1)S(1)}, bf16[8,128,256]{2,1,0:T(8,128)(2,1)S(1)}, u32[]{:S(2)}, u32[]{:S(2)}) %collective-permute-start.4) | collective-permute-done | bytes 524320 | tf_op jit(solution)/shard_map/ppermute | solution.py:45
  41.2 1.6 fusion.56
  42.8 1.3 copy.25
  44.1 2.2 fusion.14
  46.4 2.4 convolution_convert_fusion.2
  48.8 14.3 %all_gather.13 = bf16[256,1024]{1,0:T(8,128)(2,1)S(1)} all-gather(bf16[256,128]{1,0:T(8,128)(2,1)S(1)} %convolution_convert_fusion.2), channel_id=1, replica_groups=mesh['ctx'=4,'tp'=8] {'tp'}, dimensions={1}, use_global_device_ids=true | all-gather | bytes 589824 | tf_op jit(solution)/shard_map/all_gather | solution.py:97
  63.1 0.9 fusion.57
  64.7 3.5 %fusion.37 = f32[256,512]{1,0:T(8,128)S(1)} fusion(bf16[4096,512]{1,0:T(8,128)(2,1)} %param.17, bf16[256,4096]{1,0:T(8,128)(2,1)S(1)} %copy-done.2, f32[4096]{0:T(1024)S(1)} %convert_element_type.76, f32[256]{0:T(256)S(1)} %add_rsqrt_fusion.1), kind=kOutput, calls=%fused_computation.43 | convolution fusion | flops 1077936128 | bytes 6833152 | tf_op jit(solution)/shard_map/dot_general | solution.py:90
  68.4 1.2 reshape.161
  70.3 1.0 multiply_subtract_fusion
  71.5 1.0 subtract_convert_fusion
  72.6 8.7 %fusion.30 = f32[4352,256,4]{1,0,2:T(8,128)} fusion(bf16[256,128]{1,0:T(8,128)(2,1)S(1)} %dynamic-slice_bitcast_fusion, bf16[4096,128]{1,0:T(8,128)(2,1)S(1)} %bitcast.65, bf16[256,4,64]{2,0,1:T(8,128)(2,1)S(1)} %get-tuple-element.9, bf16[256,4,64]{2,0,1:T(8,128)(2,1)S(1)} %get-tuple-element.8), kind=kOutput, calls=%fused_computation.39 | convolution fusion | flops 1143603200 | bytes 19202048 | tf_op jit(solution)/shard_map/chd,kd->hck/dot_general | solution.py:115
  81.3 18.8 %fusion.60 = (f32[4,256]{1,0:T(4,128)S(1)}, bf16[4,256,4352]{1,2,0:T(8,128)(2,1)}) fusion(f32[4352,256,4]{1,0,2:T(8,128)} %fusion.30, pred[256,4352]{0,1:T(8,128)(4,1)} %pad_add_fusion), kind=kOutput, calls=%fused_computation.91 | output fusion | flops 31199488 | bytes 27856896 | tf_op jit(solution)/shard_map/sub | solution.py:119
  100.1 5.3 %fusion.25 = bf16[256,4,128]{0,2,1:T(8,128)(2,1)S(1)} fusion(bf16[4,256,4352]{1,2,0:T(8,128)(2,1)} %get-tuple-element.21, bf16[256,128]{0,1:T(8,128)(2,1)S(1)} %copy-done.9, bf16[4096,128]{0,1:T(8,128)(2,1)} %copy.25, f32[256,4]{0,1:T(4,128)S(1)} %bitcast.72), kind=kOutput, calls=%fused_computation.33 | convolution fusion | flops 1143341056 | bytes 10293248 | tf_op jit(solution)/shard_map/hck,kd->hcd/dot_general | solution.py:121
  105.4 2.7 convolution_convert_fusion
  108.2 149.9 %all-gather.6.cloned.1.call-done = bf16[2048,4096]{1,0:T(8,128)(2,1)} async-done(((bf16[256,4096]{1,0:T(8,128)(2,1)}), bf16[2048,4096]{1,0:T(8,128)(2,1)}) %all-gather.6.cloned.1.call-update) | async-done | bytes 16777232 | tf_op jit(solution)/shard_map/all_gather | solution.py:132
  258.1 10.5 %reduce_sum.41 = bf16[256,4096]{1,0:T(8,128)(2,1)} reduce(bf16[8,256,4096]{2,1,0:T(8,128)(2,1)} %bitcast.64, bf16[]{:T(256)} %constant.67.clone.1), dimensions={0}, to_apply=%region_3.4 | reduce | flops 7340032 | bytes 18874370 | tf_op jit(solution)/shard_map/reduce_sum | solution.py:132
  268.6 2.5 fusion.11
  271.1 1.3 copy-done.5
  272.4 6.3 %fusion.35 = f32[256,1376]{0,1:T(8,128)S(1)} fusion(bf16[4096,1376]{0,1:T(8,128)(2,1)} %param.20, bf16[256,4096]{1,0:T(8,128)(2,1)S(1)} %get-tuple-element.3, f32[4096]{0:T(1024)S(1)} %convert_element_type.89, f32[256]{0:T(256)S(1)} %add_rsqrt_fusion), kind=kOutput, calls=%fused_computation.42 | convolution fusion | flops 2889875456 | bytes 14795776 | tf_op jit(solution)/shard_map/dot_general | solution.py:140
  278.8 21.7 %fusion.10 = bf16[4096,256]{0,1:T(8,128)(2,1)} fusion(bf16[1376,4096]{1,0:T(8,128)(2,1)} %param.22, bf16[4096,1376]{0,1:T(8,128)(2,1)} %param.21, f32[256,1376]{0,1:T(8,128)S(1)} %fusion.35, bf16[256,4096]{1,0:T(8,128)(2,1)} %copy-done.5, f32[4096]{0:T(1024)S(1)} %convert_element_type.89, f32[256]{0:T(256)S(1)} %add_rsqrt_fusion), kind=kOutput, calls=%fused_computation.19 | convolution fusion | flops 5778718720 | bytes 28165120 | tf_op jit(solution)/shard_map/dot_general | solution.py:36
  301.5 33.3 %reduce-scatter.2.cloned.1.call-done = bf16[512,256]{0,1:T(8,128)(2,1)} async-done(((bf16[4096,256]{0,1:T(8,128)(2,1)}), bf16[512,256]{0,1:T(8,128)(2,1)}) %reduce-scatter.2.cloned.1.call-update) | async-done | bytes 262160 | tf_op jit(solution)/shard_map/reduce_scatter | solution.py:143
  334.7 1.8 fusion.41
  (60 shorter events, 8.5 us)
Async XLA Ops:
  7.2 39.2 %copy-start = (bf16[4096,128]{1,0:T(8,128)(2,1)S(1)}, bf16[4096,128]{1,0:T(8,128)(2,1)}, u32[]{:S(2)}) copy-start(bf16[4096,128]{1,0:T(8,128)(2,1)} %param.18) | copy-start | bytes 3145732
  7.2 36.9 %all-gather.4.cloned.1.call-start = ((), (), s32[]{:S(2)}) async-start(), calls=%async_computation.1 | async-start | bytes 2359296 | tf_op jit(solution)/shard_map/all_gather | solution.py:87
  7.9 250.1 %all-gather.6.cloned.1.call-start = ((), (), s32[]{:S(2)}) async-start(), calls=%async_computation.3 | async-start | bytes 18874368 | tf_op jit(solution)/shard_map/all_gather | solution.py:132
  8.6 15.9 %collective-permute-start.2 = (s32[2,8]{1,0:T(2,128)S(1)}, s32[2,8]{1,0:T(2,128)S(1)}, u32[]{:S(2)}, u32[]{:S(2)}) collective-permute-start(s32[2,8]{1,0:T(2,128)S(1)} %pad_add_fusion.1), channel_id=1, source_target_pairs={{0,24},{8,0},{16,8},{24,16},{1,25},{9,1},{17,9},{25,17},{2,26},{10... | collective-permute-start | bytes 200 | tf_op jit(solution)/shard_map/ppermute | solution.py:45
  12.5 12.0 %collective-permute-start.1 = (s32[2,8]{1,0:T(2,128)S(1)}, s32[2,8]{1,0:T(2,128)S(1)}, u32[]{:S(2)}, u32[]{:S(2)}) collective-permute-start(s32[2,8]{1,0:T(2,128)S(1)} %pad_add_fusion.1), channel_id=1, source_target_pairs={{0,16},{8,24},{16,0},{24,8},{1,17},{9,25},{17,1},{25,9},{2,18},{10... | collective-permute-start | bytes 200 | tf_op jit(solution)/shard_map/ppermute | solution.py:45
  13.0 11.5 %collective-permute-start = (s32[2,8]{1,0:T(2,128)S(1)}, s32[2,8]{1,0:T(2,128)S(1)}, u32[]{:S(2)}, u32[]{:S(2)}) collective-permute-start(s32[2,8]{1,0:T(2,128)S(1)} %pad_add_fusion.1), channel_id=1, source_target_pairs={{0,8},{8,16},{16,24},{24,0},{1,9},{9,17},{17,25},{25,1},{2,10},{10... | collective-permute-start | bytes 200 | tf_op jit(solution)/shard_map/ppermute | solution.py:45
  14.8 16.4 %collective-permute-start.5 = (bf16[8,128,256]{2,1,0:T(8,128)(2,1)S(1)}, bf16[8,128,256]{2,1,0:T(8,128)(2,1)S(1)}, u32[]{:S(2)}, u32[]{:S(2)}) collective-permute-start(bf16[8,128,256]{2,1,0:T(8,128)(2,1)S(1)} %pad_maximum_fusion.1), channel_id=1, source_target_pairs={{0,24},{8,0},{16,8},{24,16},{1,25},{9,1},{17,9},{25,17},{2,26},{10... | collective-permute-start | bytes 1572872 | tf_op jit(solution)/shard_map/ppermute | solution.py:45
  17.2 23.8 %collective-permute-start.4 = (bf16[8,128,256]{2,1,0:T(8,128)(2,1)S(1)}, bf16[8,128,256]{2,1,0:T(8,128)(2,1)S(1)}, u32[]{:S(2)}, u32[]{:S(2)}) collective-permute-start(bf16[8,128,256]{2,1,0:T(8,128)(2,1)S(1)} %pad_maximum_fusion.1), channel_id=1, source_target_pairs={{0,16},{8,24},{16,0},{24,8},{1,17},{9,25},{17,1},{25,9},{2,18},{10... | collective-permute-start | bytes 1572872 | tf_op jit(solution)/shard_map/ppermute | solution.py:45
  24.5 16.4 %collective-permute-start.3 = (bf16[8,128,256]{2,1,0:T(8,128)(2,1)S(1)}, bf16[8,128,256]{2,1,0:T(8,128)(2,1)S(1)}, u32[]{:S(2)}, u32[]{:S(2)}) collective-permute-start(bf16[8,128,256]{2,1,0:T(8,128)(2,1)S(1)} %pad_maximum_fusion.1), channel_id=1, source_target_pairs={{0,8},{8,16},{16,24},{24,0},{1,9},{9,17},{17,25},{25,1},{2,10},{10... | collective-permute-start | bytes 1572872 | tf_op jit(solution)/shard_map/ppermute | solution.py:45
  44.1 20.6 %copy-start.2 = (bf16[256,4096]{1,0:T(8,128)(2,1)S(1)}, bf16[256,4096]{1,0:T(8,128)(2,1)}, u32[]{:S(2)}) copy-start(bf16[256,4096]{1,0:T(8,128)(2,1)} %all-gather.4.cloned.1.call-done) | copy-start | bytes 6291460
  69.6 3.0 copy-start.4
  71.3 9.9 %copy-start.6 = (bf16[256,4,64]{2,0,1:T(8,128)(2,1)}, bf16[256,4,64]{2,0,1:T(8,128)(2,1)S(1)}, u32[]{:S(2)}) copy-start(bf16[256,4,64]{2,0,1:T(8,128)(2,1)S(1)} %get-tuple-element.11) | copy-start | bytes 393220
  81.3 18.8 %copy-start.9 = (bf16[256,128]{0,1:T(8,128)(2,1)S(1)}, bf16[256,128]{0,1:T(8,128)(2,1)}, u32[]{:S(2)}) copy-start(bf16[256,128]{0,1:T(8,128)(2,1)} %copy.21) | copy-start | bytes 196612
  100.1 5.3 %copy-start.3 = (bf16[512,4096]{1,0:T(8,128)(2,1)S(1)}, bf16[512,4096]{1,0:T(8,128)(2,1)}, u32[]{:S(2)}) copy-start(bf16[512,4096]{1,0:T(8,128)(2,1)} %param.19) | copy-start | bytes 12582916
  105.4 2.7 copy-start.10
  108.1 226.7 %reduce-scatter.2.cloned.1.call-start = ((), (), s32[]{:S(2)}) async-start(), calls=%async_computation.2 | async-start | bytes 2359296 | tf_op jit(solution)/shard_map/reduce_scatter | solution.py:143
  271.1 1.3 copy-start.5
  278.8 21.8 %copy-start.7 = (bf16[256,4,64]{2,0,1:T(8,128)(2,1)S(1)}, bf16[256,4,64]{2,0,1:T(8,128)(2,1)}, u32[]{:S(2)}) copy-start(bf16[256,4,64]{2,0,1:T(8,128)(2,1)} %copy-done.6) | copy-start | bytes 393220
  278.8 21.9 %copy-start.8 = (bf16[256,512]{1,0:T(8,128)(2,1)S(1)}, bf16[256,512]{1,0:T(8,128)(2,1)}, u32[]{:S(2)}) copy-start(bf16[256,512]{1,0:T(8,128)(2,1)} %get-tuple-element.12) | copy-start | bytes 786436
  278.8 57.8 %copy-start.1 = (bf16[4096,128]{1,0:T(8,128)(2,1)S(1)}, bf16[4096,128]{1,0:T(8,128)(2,1)}, u32[]{:S(2)}) copy-start(bf16[4096,128]{1,0:T(8,128)(2,1)} %param.18) | copy-start | bytes 3145732
Sparse Core Ops, SparseCore 0:
  9.6 31.7 all-gather.3
  108.2 149.8 all-gather.5
  300.7 33.9 reduce-scatter.1
